TPU v7x, 512 devices: a whole 4x8x8 slice. The times are simulated.
512 devices in a mesh: dp: 32 (over z, x), fsdp: 16 (over y, core).
Axes of the slice: x: 4, y: 8, z: 8, core: 2. Of those that a mesh axis runs over, the one named last changes fastest.
Arguments:
- projected: bfloat16 [65536, 2304], P(('dp', 'fsdp')), may hold values from -7.03125 to 7.03125
- out_weight: bfloat16 [768, 1536], P('fsdp'), may hold values from -0.21875 to 0.21875
- kernel: float32 [31, 1536], replicated, may hold values from -2 to 2
- cotangent: bfloat16 [65536, 1536], P(('dp', 'fsdp')), may hold values from -6 to 6
- send_rows: int32 [65536], P(('dp', 'fsdp')), may hold values from -1 to 127, as said below
- compute_src: int32 [65536], P(('dp', 'fsdp')), may hold values from -1 to 127, as said below
- segment: int32 [65536], P(('dp', 'fsdp')), may hold values from -1 to 3, as said below
Outputs:
- block_out: bfloat16 [65536, 1536], P(('dp', 'fsdp'))
- projected_grad: bfloat16 [65536, 2304], P(('dp', 'fsdp'))
- out_weight_grad: float32 [768, 1536], P('fsdp')
- kernel_grad: float32 [31, 1536], replicated
Inputs may be any that keep to these rules, and one draw needn't show every extreme that they name: `send_rows`: A device's 128 entries are 32 blocks of 4, block t for index t of dp at the same fsdp index; each lists rows of the device's own block of projected, each row at most once, filled entries first in a block and -1 after them. In every draw some device of each fsdp index fills all its entries. `compute_src`: on device (t, f), a row holds s * 4 + k when it receives entry t * 4 + k of device (s, f); every filled entry of send_rows is received by exactly one row, and a row holds -1 when it receives nothing. Filled rows come first. In every draw some device of each fsdp index receives a full block from every device. On each device, rows with compute_src = -1 hold -1, the others hold segment numbers from 0 that never fall along the rows.
All inputs are finite; a program needn't handle non-finite values.
Results may differ from a plain program's by a relative error of at most 0.018.
Values may be sent and summed in bfloat16 or wider, within the bound.
No kernel may reach another device: no remote copies, remote signals or barrier semaphores. Data moves between devices by JAX's collectives and lax.ppermute only.
A program may use at most 128 MiB of HBM per device.

v0:
```python
import jax
import jax.numpy as jnp
from jax import lax
from jax.sharding import Mesh, PartitionSpec as P

DP = ("dz", "dx")
FSDP = ("fy", "fc")
HEADS = 8
HEAD_DIM = 96


def split_heads(frames):
    length = frames.shape[0]
    inner_width = HEADS * HEAD_DIM
    query_part = frames[:, :inner_width].reshape(length, HEADS, HEAD_DIM)
    key_part = frames[:, inner_width : 2 * inner_width].reshape(length, HEADS, HEAD_DIM)
    value_part = frames[:, 2 * inner_width :].reshape(length, HEADS, HEAD_DIM)
    return (query_part, key_part, value_part)


def attend(frames, segment):
    query_part, key_part, value_part = split_heads(frames)
    scores = jnp.einsum(
        "qhd,khd->hqk", query_part, key_part, preferred_element_type=jnp.float32
    ) * HEAD_DIM ** (-0.5)
    inside = segment[:, None] == segment[None, :]
    scores = jnp.where(inside[None], scores, -1e30)
    highest = jnp.max(scores, axis=2, keepdims=True)
    weights = jnp.exp(scores - highest)
    soft_probs = weights / jnp.sum(weights, axis=2, keepdims=True)
    rounded = soft_probs.astype(jnp.bfloat16)
    context = jnp.einsum("hqk,khd->qhd", rounded, value_part, preferred_element_type=jnp.float32)
    return (
        context.reshape(frames.shape[0], HEADS * HEAD_DIM).astype(jnp.bfloat16),
        soft_probs,
        rounded,
    )


def attend_back(frames, soft_probs, rounded, context_grad):
    query_part, key_part, value_part = split_heads(frames)
    length = frames.shape[0]
    inner_width = HEADS * HEAD_DIM
    upstream = context_grad.reshape(length, HEADS, HEAD_DIM)
    value_grad = jnp.einsum("hqk,qhd->khd", rounded, upstream, preferred_element_type=jnp.float32)
    prob_grad = jnp.einsum("qhd,khd->hqk", upstream, value_part, preferred_element_type=jnp.float32)
    score_grad = soft_probs * (prob_grad - jnp.sum(prob_grad * soft_probs, axis=2, keepdims=True))
    score_grad = (score_grad * HEAD_DIM ** (-0.5)).astype(jnp.bfloat16)
    query_grad = jnp.einsum(
        "hqk,khd->qhd", score_grad, key_part, preferred_element_type=jnp.float32
    )
    key_grad = jnp.einsum(
        "hqk,qhd->khd", score_grad, query_part, preferred_element_type=jnp.float32
    )
    return jnp.concatenate(
        [
            query_grad.reshape(length, inner_width).astype(jnp.bfloat16),
            key_grad.reshape(length, inner_width).astype(jnp.bfloat16),
            value_grad.reshape(length, inner_width).astype(jnp.bfloat16),
        ],
        axis=1,
    )


def finish(mixed, kernel, segment):
    length = mixed.shape[0]
    tap_count = kernel.shape[0]
    half_span = (tap_count - 1) // 2
    signal = mixed.astype(jnp.float32)
    padded = jnp.pad(signal, ((half_span, half_span), (0, 0)))
    neighbours = jnp.pad(segment, (half_span, half_span), constant_values=-2)
    convolved = jnp.zeros_like(signal)
    for offset in range(tap_count):
        matching = (neighbours[offset : offset + length] == segment).astype(jnp.float32)
        convolved = (
            convolved + kernel[offset] * padded[offset : offset + length] * matching[:, None]
        )
    return signal + jax.nn.silu(convolved)


def body(projected, out_weight, kernel, cotangent, send_rows, compute_src, segment):
    row_count = projected.shape[0]
    present = send_rows >= 0
    outgoing = jnp.take(projected, jnp.maximum(send_rows, 0), axis=0)
    outgoing = jnp.where(present[:, None], outgoing, jnp.zeros_like(outgoing))
    incoming = lax.all_to_all(outgoing, DP, split_axis=0, concat_axis=0, tiled=True)
    filled = compute_src >= 0
    frames = jnp.take(incoming, jnp.maximum(compute_src, 0), axis=0)
    frames = jnp.where(filled[:, None], frames, jnp.zeros_like(frames))
    context, soft_probs, rounded = attend(frames, segment)
    columns = context
    mixed_sums = jnp.dot(
        columns,
        lax.all_gather(out_weight, FSDP, axis=0, tiled=True),
        preferred_element_type=jnp.float32,
    )
    mixed = mixed_sums.astype(jnp.bfloat16)
    result, pullback = jax.vjp(
        lambda signal, kernel_taps: finish(signal, kernel_taps, segment), mixed, kernel
    )
    mixed_grad, kernel_part = pullback(cotangent.astype(jnp.float32))
    columns = context
    weight_share = lax.psum_scatter(
        jnp.einsum("rc,rd->cd", columns, mixed_grad, preferred_element_type=jnp.float32).astype(
            jnp.bfloat16
        ),
        FSDP,
        scatter_dimension=0,
        tiled=True,
    ).astype(jnp.float32)
    context_grad = jnp.einsum(
        "rd,cd->rc",
        mixed_grad,
        lax.all_gather(out_weight, FSDP, axis=0, tiled=True),
        preferred_element_type=jnp.float32,
    ).astype(jnp.bfloat16)
    frame_grad = attend_back(frames, soft_probs, rounded, context_grad)
    slot_total = incoming.shape[0]
    back_index = jnp.where(filled, compute_src, slot_total)
    returning = jnp.zeros_like(incoming).at[back_index].set(frame_grad, mode="drop")
    arrived = lax.all_to_all(returning, DP, split_axis=0, concat_axis=0, tiled=True)
    source_index = jnp.where(present, send_rows, row_count)
    projected_grad = jnp.zeros_like(projected).at[source_index].set(arrived, mode="drop")
    scale_factor = (row_count * lax.axis_size(DP) * lax.axis_size(FSDP)) ** (-0.5)
    weight_share, arrived = lax.optimization_barrier((weight_share, arrived))
    kernel_piece = sum_rows(kernel_part, FSDP)
    owned_rows = weight_share.shape[0]
    both = jnp.concatenate([weight_share, kernel_piece], axis=0)
    piece = sum_rows(both, DP)
    both = gather_rows(piece, DP)[: both.shape[0]]
    weight_total = both[:owned_rows]
    kernel_total = gather_rows(both[owned_rows:], FSDP)[: kernel.shape[0]]
    return (
        result.astype(jnp.bfloat16),
        projected_grad,
        weight_total * scale_factor,
        kernel_total * scale_factor,
    )


def sum_rows(x, axis):
    count = lax.axis_size(axis)
    per = -(-x.shape[0] // count)
    padded = jnp.pad(x, ((0, count * per - x.shape[0]), (0, 0)))
    got = lax.all_to_all(
        padded.reshape(count, per, x.shape[1]), axis, split_axis=0, concat_axis=0, tiled=True
    )
    return jnp.sum(got, axis=0)


def gather_rows(piece, axis):
    count = lax.axis_size(axis)
    copies = jnp.broadcast_to(piece[None], (count, *piece.shape))
    got = lax.all_to_all(copies, axis, split_axis=0, concat_axis=0, tiled=True)
    return got.reshape(count * piece.shape[0], piece.shape[1])


def solution(mesh):
    dp_count, fsdp_count = mesh.devices.shape
    fine = Mesh(
        mesh.devices.reshape(dp_count // 4, 4, fsdp_count // 2, 2), ("dz", "dx", "fy", "fc")
    )
    placed = (
        P((*DP, *FSDP), None),
        P(FSDP, None),
        P(),
        P((*DP, *FSDP), None),
        P((*DP, *FSDP)),
        P((*DP, *FSDP)),
        P((*DP, *FSDP)),
    )
    return jax.shard_map(
        body,
        mesh=fine,
        in_specs=placed,
        out_specs=(P((*DP, *FSDP), None), P((*DP, *FSDP), None), P(FSDP, None), P()),
        check_vma=False,
    )
```

profile of v0, /device:TPU:1, one launch (start us, length us, event | category | flops | bytes accessed | tf_op | source)
XLA Modules:
  0.0 211.4 jit_solution(173523416918727866)
XLA Ops:
  11.3 13.7 %all-to-all-start = ((bf16[32,4,2304]{2,1,0:T(4,128)(2,1)}), bf16[32,4,2304]{2,1,0:T(4,128)(2,1)S(1)}, u32[]{:S(2)}, u32[]{:S(2)}) async-start(bf16[32,4,2304]{2,1,0:T(4,128)(2,1)} %all_to_all.28), calls=%async_computation | async-start | bytes 1179648 | tf_op jit(solution)/shard_map/all_to_all | solution.py:86
  26.6 16.0 %all-to-all-done = bf16[32,4,2304]{2,1,0:T(4,128)(2,1)S(1)} async-done(((bf16[32,4,2304]{2,1,0:T(4,128)(2,1)}), bf16[32,4,2304]{2,1,0:T(4,128)(2,1)S(1)}, u32[]{:S(2)}, u32[]{:S(2)}) %all-to-all-start) | async-done | bytes 589856 | tf_op jit(solution)/shard_map/all_to_all | solution.py:86
  46.6 11.6 %all-gather.2.cloned.1.call-done = bf16[768,1536]{1,0:T(8,128)(2,1)} async-done(((bf16[48,1536]{1,0:T(8,128)(2,1)}), bf16[768,1536]{1,0:T(8,128)(2,1)}) %all-gather.2.cloned.1.call-update) | async-done | bytes 2359312 | tf_op jit(solution)/shard_map/all_gather | solution.py:94
  58.2 2.2 %fusion.2 = f32[128,1536]{1,0:T(8,128)S(1)} fusion(bf16[128,768]{0,1:T(8,128)(2,1)S(1)} %bitcast.38, bf16[768,1536]{1,0:T(8,128)(2,1)} %all-gather.2.cloned.1.call-done), kind=kOutput, calls=%fused_computation.8 | convolution fusion | flops 302383104 | bytes 3342336 | tf_op jit(solution)/shard_map/dot_general | solution.py:92
  60.4 7.7 %multiply_reduce_fusion.31 = (f32[1536]{0:T(1024)}, f32[1536]{0:T(1024)}, f32[1536]{0:T(1024)}, f32[1536]{0:T(1024)}, f32[1536]{0:T(1024)}, /*index=5*/f32[1536]...) fusion(f32[128,1536]{1,0:T(8,128)S(1)} %fusion.2, ...), kind=kLoop, calls=%fused_computation.99 | loop fusion | flops 25152000 | bytes 3013632 | tf_op jit(solution)/shard_map/transpose(jvp())/reduce_sum | solution.py:76
  68.2 2.3 %multiply_reduce_fusion.16 = (f32[1536]{0:T(1024)}, f32[1536]{0:T(1024)}, f32[1536]{0:T(1024)}, f32[1536]{0:T(1024)}, f32[1536]{0:T(1024)}, /*index=5*/f32[1536]...) fusion(f32[128,1536]{1,0:T(8,128)S(1)} %get-tuple-element.69, ...), kind=kLoop, calls=%fused_computation.84 | loop fusion | flops 5294592 | bytes 2424832 | tf_op jit(solution)/shard_map/transpose(jvp())/reduce_sum | solution.py:76
  72.5 2.6 %multiply_reduce_fusion.4 = (f32[1536]{0:T(1024)}, f32[1536]{0:T(1024)}, f32[1536]{0:T(1024)}, f32[1536]{0:T(1024)}, f32[128,1536]{1,0:T(8,128)S(1)}, /*index=5*...) fusion(f32[128,1536]{1,0:T(8,128)S(1)} %get-tuple-element.69, ...), kind=kLoop, calls=%fused_computation.72 | loop fusion | flops 5105664 | bytes 7535616 | tf_op jit(solution)/shard_map/transpose(jvp())/reduce_sum | solution.py:76
  75.1 2.6 %pad_add_fusion = f32[158,1536]{1,0:T(8,128)S(1)} fusion(f32[128,1536]{1,0:T(8,128)S(1)} %get-tuple-element.78, f32[128,1536]{1,0:T(8,128)S(1)} %get-tuple-element.80, f32[128,1536]{1,0:T(8,128)S(1)} %get-tuple-element.81, f32[128,1536]{1,0:T(8,128)S(1)} %get-tuple-element.82, f32[128,1536]{1,0:T(8,128)S(1)} %get-tuple-element.83, ...), kind=kLoop, calls=%fused_computation.59 | loop fusion | flops 5824512 | bytes 20631552 | tf_op jit(solution)/shard_map/transpose(jvp())/add_any | solution.py:76
  78.6 2.2 %convolution_convert_fusion = bf16[768,1536]{1,0:T(8,128)(2,1)} fusion(bf16[128,768]{0,1:T(8,128)(2,1)S(1)} %bitcast.39, bf16[128,1536]{1,0:T(8,128)(2,1)S(1)} %fusion.16), kind=kOutput, calls=%fused_computation.6 | convolution fusion | flops 303169536 | bytes 2949120 | tf_op jit(solution)/shard_map/rc,rd->cd/dot_general | solution.py:104
  81.1 2.0 multiply_reduce_fusion.22
  84.7 4.6 %all-to-all-start.2 = ((f32[16,2,1536]{2,1,0:T(2,128)}), f32[16,2,1536]{2,1,0:T(2,128)S(1)}, u32[]{:S(2)}, u32[]{:S(2)}) async-start(f32[16,2,1536]{2,1,0:T(2,128)} %reshape.309), calls=%async_computation.3 | async-start | bytes 393216 | tf_op jit(solution)/shard_map/all_to_all | solution.py:145
  89.3 2.5 %convolution_convert_fusion.5 = bf16[128,768]{1,0:T(8,128)(2,1)S(1)} fusion(bf16[128,1536]{1,0:T(8,128)(2,1)S(1)} %fusion.16, bf16[768,1536]{1,0:T(8,128)(2,1)} %all-gather.2.cloned.1.call-done), kind=kOutput, calls=%fused_computation.54 | convolution fusion | flops 302088192 | bytes 2949120 | tf_op jit(solution)/shard_map/rd,cd->rc/dot_general | solution.py:111
  93.8 1.6 convolution_convert_fusion.3
  95.5 1.6 convolution_convert_fusion.4
  97.3 1.8 scatter_custom_fusion
  100.0 10.0 %all-to-all-start.1 = ((bf16[32,4,2304]{2,1,0:T(4,128)(2,1)}), bf16[32,4,2304]{2,1,0:T(4,128)(2,1)S(1)}, u32[]{:S(2)}, u32[]{:S(2)}) async-start(bf16[32,4,2304]{2,1,0:T(4,128)(2,1)} %all_to_all.31), calls=%async_computation.1 | async-start | bytes 1179648 | tf_op jit(solution)/shard_map/all_to_all | solution.py:121
  110.1 17.9 %all-to-all-done.1 = bf16[32,4,2304]{2,1,0:T(4,128)(2,1)S(1)} async-done(((bf16[32,4,2304]{2,1,0:T(4,128)(2,1)}), bf16[32,4,2304]{2,1,0:T(4,128)(2,1)S(1)}, u32[]{:S(2)}, u32[]{:S(2)}) %all-to-all-start.1) | async-done | bytes 589856 | tf_op jit(solution)/shard_map/all_to_all | solution.py:121
  128.2 12.4 %reduce-scatter.2.cloned.1.call-done = bf16[48,1536]{1,0:T(8,128)(2,1)} async-done(((bf16[768,1536]{1,0:T(8,128)(2,1)}), bf16[48,1536]{1,0:T(8,128)(2,1)}) %reduce-scatter.2.cloned.1.call-update) | async-done | bytes 147472 | tf_op jit(solution)/shard_map/reduce_scatter | solution.py:103
  141.8 20.6 %all_to_all.44 = f32[32,2,1536]{2,1,0:T(2,128)S(1)} all-to-all(f32[32,2,1536]{2,1,0:T(2,128)S(1)} %reshape.310), channel_id=1, replica_groups=mesh['dz'=8,'dx'=4,'fy'=8,'fc'=2] {'dz','dx'}, dimensions={0} | all-to-all | bytes 786432 | tf_op jit(solution)/shard_map/all_to_all | solution.py:145
  163.3 4.1 %all-to-all-start.4 = ((f32[32,2,1536]{2,1,0:T(2,128)}), f32[32,2,1536]{2,1,0:T(2,128)S(1)}, u32[]{:S(2)}, u32[]{:S(2)}) async-start(f32[32,2,1536]{2,1,0:T(2,128)} %broadcast_in_dim.55), calls=%async_computation.5 | async-start | bytes 786432 | tf_op jit(solution)/shard_map/all_to_all | solution.py:154
  167.4 2.4 %scatter_custom_fusion.1 = bf16[128,2304]{1,0:T(8,128)(2,1)} fusion(s32[128]{0:T(128)} %get-tuple-element.108, bf16[128,2304]{1,0:T(8,128)(2,1)S(1)} %reshape.340, bf16[]{:T(256)} %constant.10.clone.1), kind=kCustom, calls=%fused_computation.145 | custom fusion | bytes 590336 | tf_op jit(solution)/shard_map/scatter | solution.py:123
  169.8 9.1 %all-to-all-done.4 = f32[32,2,1536]{2,1,0:T(2,128)S(1)} async-done(((f32[32,2,1536]{2,1,0:T(2,128)}), f32[32,2,1536]{2,1,0:T(2,128)S(1)}, u32[]{:S(2)}, u32[]{:S(2)}) %all-to-all-start.4) | async-done | bytes 393248 | tf_op jit(solution)/shard_map/all_to_all | solution.py:154
  179.6 13.8 %all-to-all-start.5 = ((f32[16,2,1536]{2,1,0:T(2,128)}), f32[16,2,1536]{2,1,0:T(2,128)S(1)}, u32[]{:S(2)}, u32[]{:S(2)}) async-start(f32[16,2,1536]{2,1,0:T(2,128)} %broadcast_in_dim.57), calls=%async_computation.6 | async-start | bytes 393216 | tf_op jit(solution)/shard_map/all_to_all | solution.py:154
  194.5 9.3 %all-to-all-done.5 = f32[16,2,1536]{2,1,0:T(2,128)S(1)} async-done(((f32[16,2,1536]{2,1,0:T(2,128)}), f32[16,2,1536]{2,1,0:T(2,128)S(1)}, u32[]{:S(2)}, u32[]{:S(2)}) %all-to-all-start.5) | async-done | bytes 196640 | tf_op jit(solution)/shard_map/all_to_all | solution.py:154
  (184 shorter events, 21.6 us)
Async XLA Ops:
  7.2 51.1 %all-gather.2.cloned.1.call-start = ((), (), s32[]{:S(2)}) async-start(), calls=%async_computation.7 | async-start | bytes 2506752 | tf_op jit(solution)/shard_map/all_gather | solution.py:94
  10.1 14.9 %copy-start.4 = (f32[31,1536]{1,0:T(8,128)S(1)}, f32[31,1536]{1,0:T(8,128)}, u32[]{:S(2)}) copy-start(f32[31,1536]{1,0:T(8,128)} %param.11) | copy-start | bytes 571396
  10.2 15.1 %copy-start.46 = (s32[128]{0:T(128)S(1)}, s32[128]{0:T(128)}, u32[]{:S(2)}) copy-start(s32[128]{0:T(128)} %param.14) | copy-start | bytes 1540
  10.2 16.0 %copy-start.44 = (s32[128]{0:T(128)S(1)}, s32[128]{0:T(128)}, u32[]{:S(2)}) copy-start(s32[128]{0:T(128)} %param.15) | copy-start | bytes 1540
  11.3 31.2 %all-to-all-start = ((bf16[32,4,2304]{2,1,0:T(4,128)(2,1)}), bf16[32,4,2304]{2,1,0:T(4,128)(2,1)S(1)}, u32[]{:S(2)}, u32[]{:S(2)}) async-start(bf16[32,4,2304]{2,1,0:T(4,128)(2,1)} %all_to_all.28), calls=%async_computation | async-start | bytes 1179648 | tf_op jit(solution)/shard_map/all_to_all | solution.py:86
  25.0 115.5 %reduce-scatter.2.cloned.1.call-start = ((), (), s32[]{:S(2)}) async-start(), calls=%async_computation.8 | async-start | bytes 2506752 | tf_op jit(solution)/shard_map/reduce_scatter | solution.py:103
  26.4 44.6 %copy-start.38 = (f32[128]{0:T(128)}, f32[128]{0:T(128)S(1)}, u32[]{:S(2)}) copy-start(f32[128]{0:T(128)S(1)} %get-tuple-element.122) | copy-start | bytes 1540
  26.4 44.6 %copy-start.40 = (f32[128]{0:T(128)}, f32[128]{0:T(128)S(1)}, u32[]{:S(2)}) copy-start(f32[128]{0:T(128)S(1)} %get-tuple-element.123) | copy-start | bytes 1540
  26.4 44.6 %copy-start.42 = (f32[128]{0:T(128)}, f32[128]{0:T(128)S(1)}, u32[]{:S(2)}) copy-start(f32[128]{0:T(128)S(1)} %get-tuple-element.124) | copy-start | bytes 1540
  26.4 45.3 %copy-start.26 = (f32[128]{0:T(128)}, f32[128]{0:T(128)S(1)}, u32[]{:S(2)}) copy-start(f32[128]{0:T(128)S(1)} %get-tuple-element.116) | copy-start | bytes 1540
  26.4 45.3 %copy-start.28 = (f32[128]{0:T(128)}, f32[128]{0:T(128)S(1)}, u32[]{:S(2)}) copy-start(f32[128]{0:T(128)S(1)} %get-tuple-element.117) | copy-start | bytes 1540
  26.4 45.3 %copy-start.30 = (f32[128]{0:T(128)}, f32[128]{0:T(128)S(1)}, u32[]{:S(2)}) copy-start(f32[128]{0:T(128)S(1)} %get-tuple-element.118) | copy-start | bytes 1540
  26.4 45.3 %copy-start.32 = (f32[128]{0:T(128)}, f32[128]{0:T(128)S(1)}, u32[]{:S(2)}) copy-start(f32[128]{0:T(128)S(1)} %get-tuple-element.119) | copy-start | bytes 1540
  26.4 45.3 %copy-start.34 = (f32[128]{0:T(128)}, f32[128]{0:T(128)S(1)}, u32[]{:S(2)}) copy-start(f32[128]{0:T(128)S(1)} %get-tuple-element.120) | copy-start | bytes 1540
  26.5 45.3 %copy-start.36 = (f32[128]{0:T(128)}, f32[128]{0:T(128)S(1)}, u32[]{:S(2)}) copy-start(f32[128]{0:T(128)S(1)} %get-tuple-element.121) | copy-start | bytes 1540
  26.6 19.0 %copy-start.25 = (pred[128,128]{0,1:T(8,128)(4,1)}, pred[128,128]{0,1:T(8,128)(4,1)S(1)}, u32[]{:S(2)}) copy-start(pred[128,128]{0,1:T(8,128)(4,1)S(1)} %broadcast_compare_fusion) | copy-start | bytes 49156
  44.2 14.1 %copy-start.2 = (bf16[128,768]{0,1:T(8,128)(2,1)}, bf16[128,768]{0,1:T(8,128)(2,1)S(1)}, u32[]{:S(2)}) copy-start(bf16[128,768]{0,1:T(8,128)(2,1)S(1)} %copy.46) | copy-start | bytes 589828
  46.6 13.8 %copy-start.1 = (bf16[128,1536]{1,0:T(8,128)(2,1)S(1)}, bf16[128,1536]{1,0:T(8,128)(2,1)}, u32[]{:S(2)}) copy-start(bf16[128,1536]{1,0:T(8,128)(2,1)} %param.12) | copy-start | bytes 1179652
  83.5 8.5 %copy-start.3 = (bf16[128,768]{0,1:T(8,128)(2,1)S(1)}, bf16[128,768]{0,1:T(8,128)(2,1)}, u32[]{:S(2)}) copy-start(bf16[128,768]{0,1:T(8,128)(2,1)} %copy-done.2) | copy-start | bytes 589828
  83.6 8.5 %copy-start.48 = (f32[8,128]{1,0:T(8,128)S(1)}, f32[8,128]{1,0:T(8,128)}, u32[]{:S(2)}) copy-start(f32[8,128]{1,0:T(8,128)} %copy-done.47) | copy-start | bytes 12292
  84.7 15.3 %all-to-all-start.2 = ((f32[16,2,1536]{2,1,0:T(2,128)}), f32[16,2,1536]{2,1,0:T(2,128)S(1)}, u32[]{:S(2)}, u32[]{:S(2)}) async-start(f32[16,2,1536]{2,1,0:T(2,128)} %reshape.309), calls=%async_computation.3 | async-start | bytes 393216 | tf_op jit(solution)/shard_map/all_to_all | solution.py:145
  100.0 28.1 %all-to-all-start.1 = ((bf16[32,4,2304]{2,1,0:T(4,128)(2,1)}), bf16[32,4,2304]{2,1,0:T(4,128)(2,1)S(1)}, u32[]{:S(2)}, u32[]{:S(2)}) async-start(bf16[32,4,2304]{2,1,0:T(4,128)(2,1)} %all_to_all.31), calls=%async_computation.1 | async-start | bytes 1179648 | tf_op jit(solution)/shard_map/all_to_all | solution.py:121
  163.3 15.6 %all-to-all-start.4 = ((f32[32,2,1536]{2,1,0:T(2,128)}), f32[32,2,1536]{2,1,0:T(2,128)S(1)}, u32[]{:S(2)}, u32[]{:S(2)}) async-start(f32[32,2,1536]{2,1,0:T(2,128)} %broadcast_in_dim.55), calls=%async_computation.5 | async-start | bytes 786432 | tf_op jit(solution)/shard_map/all_to_all | solution.py:154
  179.6 24.2 %all-to-all-start.5 = ((f32[16,2,1536]{2,1,0:T(2,128)}), f32[16,2,1536]{2,1,0:T(2,128)S(1)}, u32[]{:S(2)}, u32[]{:S(2)}) async-start(f32[16,2,1536]{2,1,0:T(2,128)} %broadcast_in_dim.57), calls=%async_computation.6 | async-start | bytes 393216 | tf_op jit(solution)/shard_map/all_to_all | solution.py:154
  (32 other events, 78.0 us)
Sparse Core Ops, SparseCore 0:
  10.1 48.0 all-gather.1
  81.0 59.5 reduce-scatter.1
where the time goes:
time: 212 us; the launch traced here: 211 us
  waiting for transfers between devices  76.9 us (36%)
  starting transfers between devices  46.4 us (22%)
  other arithmetic  26.2 us (12%)
  blocking collectives  20.6 us (10%)
  between operations  15.3 us (7%)
  matrix products  13.3 us (6%)
  local copies, waits for them, and re-layouts  12.8 us (6%)
    all_to_all x1, blocking collectives, sum_rows(): lax.all_to_all(padded.reshape(count, per, x.shape[1]), axis, split_axis=0...  20.6 us
    all_to_all x2, waiting for transfers between devices, gather_rows(): got = lax.all_to_all(copies, axis, split_axis=0, concat_axis=0, tiled=True)  18.4 us
    all_to_all x2, starting transfers between devices, gather_rows(): got = lax.all_to_all(copies, axis, split_axis=0, concat_axis=0, tiled=True)  17.9 us
    all_to_all x1, waiting for transfers between devices, body(): lax.all_to_all(returning, DP, split_axis=0, concat_axis=0, tiled=True)  17.9 us
    all_to_all x1, waiting for transfers between devices, body(): lax.all_to_all(outgoing, DP, split_axis=0, concat_axis=0, tiled=True)  16 us
    reduce_sum x4, other arithmetic, finish(): kernel[offset] * padded[offset:offset + length] * matching[:, None]  14.6 us
    all_to_all x1, starting transfers between devices, body(): lax.all_to_all(outgoing, DP, split_axis=0, concat_axis=0, tiled=True)  13.7 us
    reduce_scatter x1, waiting for transfers between devices, body(): lax.psum_scatter(jnp.einsum('rc,rd->cd', columns, mixed_grad, preferred_e...  12.4 us
  transfers between devices with their start and end apart: 7, of which 6 were waited for; matrix products, arithmetic and copies ran while one was open for 11% of the time, Pallas kernels for 0%

commit v1 on v0

--- a/solution.py
+++ b/solution.py
@@ -91,7 +91,9 @@
     columns = context
     mixed_sums = jnp.dot(
         columns,
-        lax.all_gather(out_weight, FSDP, axis=0, tiled=True),
+        jnp.concatenate(
+            lax.all_to_all(jnp.stack([out_weight] * lax.axis_size(FSDP)), FSDP, 0, 0), axis=0
+        ),
         preferred_element_type=jnp.float32,
     )
     mixed = mixed_sums.astype(jnp.bfloat16)

time: 212 us -> 269 us (1.27)
  blocking collectives: 20.6 us -> 51.5 us
  waiting for transfers between devices: 76.9 us -> 102 us
  local copies, waits for them, and re-layouts: 12.8 us -> 21.3 us
  starting transfers between devices: 46.4 us -> 37.9 us
    all_to_all x1, waiting for transfers between devices: 16 us -> 59.4 us  [body(): lax.all_to_all(jnp.stack([out_weight] * lax.axis_size(FSDP)), FSDP, 0, 0)]
    all_to_all x0 -> x1, blocking collectives: none -> 31 us  [body(): lax.all_to_all(outgoing, DP, split_axis=0, concat_axis=0, tiled=True)]
    reduce_scatter x1, waiting for transfers between devices: 12.4 us -> 0.02 us  [body(): lax.psum_scatter(jnp.einsum('rc,rd->cd', columns, mixed_grad, preferred_e...]
    all_gather x1, waiting for transfers between devices: 11.6 us -> 0.02 us  [body(): lax.all_gather(out_weight, FSDP, axis=0, tiled=True)]
    reshape x31, local copies, waits for them, and re-layouts: 0.2 us -> 8.54 us  [finish(): kernel[offset] * padded[offset:offset + length] * matching[:, None]]
    all_to_all x1, starting transfers between devices: 10 us -> 5 us  [body(): lax.all_to_all(returning, DP, split_axis=0, concat_axis=0, tiled=True)]
    all_to_all x1, waiting for transfers between devices: 0.01 us -> 4.71 us  [sum_rows(): lax.all_to_all(padded.reshape(count, per, x.shape[1]), axis, split_axis=0...]
    all_to_all x1, starting transfers between devices: 13.7 us -> 9.71 us  [body(): lax.all_to_all(jnp.stack([out_weight] * lax.axis_size(FSDP)), FSDP, 0, 0)]
  transfers between devices with their start and end apart: 7 -> 7, of which waited for: 6 -> 5; matrix products, arithmetic and copies ran while one was open for 11% -> 20% of each run, Pallas kernels for 0% -> 0%
where the time goes in v1:
time: 269 us; the launch traced here: 268 us
  waiting for transfers between devices  102 us (38%)
  blocking collectives  51.5 us (19%)
  starting transfers between devices  37.9 us (14%)
  other arithmetic  27.5 us (10%)
  local copies, waits for them, and re-layouts  21.3 us (8%)
  between operations  14.9 us (6%)
  matrix products  13.2 us (5%)
    all_to_all x1, waiting for transfers between devices, body(): lax.all_to_all(jnp.stack([out_weight] * lax.axis_size(FSDP)), FSDP, 0, 0)  59.4 us
    all_to_all x1, blocking collectives, body(): lax.all_to_all(outgoing, DP, split_axis=0, concat_axis=0, tiled=True)  31 us
    all_to_all x1, blocking collectives, sum_rows(): lax.all_to_all(padded.reshape(count, per, x.shape[1]), axis, split_axis=0...  20.5 us
    all_to_all x2, starting transfers between devices, gather_rows(): got = lax.all_to_all(copies, axis, split_axis=0, concat_axis=0, tiled=True)  18.5 us
    all_to_all x2, waiting for transfers between devices, gather_rows(): got = lax.all_to_all(copies, axis, split_axis=0, concat_axis=0, tiled=True)  18.4 us
    all_to_all x1, waiting for transfers between devices, body(): lax.all_to_all(returning, DP, split_axis=0, concat_axis=0, tiled=True)  18.4 us
    reduce_sum x4, other arithmetic, finish(): kernel[offset] * padded[offset:offset + length] * matching[:, None]  15.2 us
    all_to_all x1, starting transfers between devices, body(): lax.all_to_all(jnp.stack([out_weight] * lax.axis_size(FSDP)), FSDP, 0, 0)  9.71 us
  transfers between devices with their start and end apart: 7, of which 5 were waited for; matrix products, arithmetic and copies ran while one was open for 20% of the time, Pallas kernels for 0%

profile of v1, /device:TPU:1, one launch (start us, length us, event | category | flops | bytes accessed | tf_op | source)
XLA Modules:
  0.0 267.9 jit_solution(16116399148430500624)
XLA Ops:
  10.4 31.0 %all_to_all.49 = bf16[32,4,2304]{2,1,0:T(4,128)(2,1)S(1)} all-to-all(bf16[32,4,2304]{2,1,0:T(4,128)(2,1)S(1)} %all_to_all.31), channel_id=1, replica_groups=mesh['dz'=8,'dx'=4,'fy'=8,'fc'=2] {'dz','dx'}, dimensions={0} | all-to-all | bytes 1179648 | tf_op jit(solution)/shard_map/all_to_all | solution.py:86
  41.4 1.7 stack.2
  43.1 9.7 %all-to-all-start.1 = ((bf16[16,48,1536]{2,1,0:T(8,128)(2,1)}), bf16[16,48,1536]{2,1,0:T(8,128)(2,1)}, u32[]{:S(2)}, u32[]{:S(2)}) async-start(bf16[16,48,1536]{2,1,0:T(8,128)(2,1)} %stack.2), calls=%async_computation.1 | async-start | bytes 4718592 | tf_op jit(solution)/shard_map/all_to_all | solution.py:95
  58.6 59.4 %all-to-all-done.1 = bf16[16,48,1536]{2,1,0:T(8,128)(2,1)} async-done(((bf16[16,48,1536]{2,1,0:T(8,128)(2,1)}), bf16[16,48,1536]{2,1,0:T(8,128)(2,1)}, u32[]{:S(2)}, u32[]{:S(2)}) %all-to-all-start.1) | async-done | bytes 2359328 | tf_op jit(solution)/shard_map/all_to_all | solution.py:95
  118.0 2.2 fusion.2
  120.2 7.7 %multiply_reduce_fusion.31 = (f32[1536]{0:T(1024)}, f32[1536]{0:T(1024)}, f32[1536]{0:T(1024)}, f32[1536]{0:T(1024)}, f32[1536]{0:T(1024)}, /*index=5*/f32[1536]...) fusion(f32[128,1536]{1,0:T(8,128)S(1)} %fusion.2, ...), kind=kLoop, calls=%fused_computation.99 | loop fusion | flops 25152000 | bytes 3013632 | tf_op jit(solution)/shard_map/transpose(jvp())/reduce_sum | solution.py:76
  128.0 2.3 multiply_reduce_fusion.16
  130.2 2.6 multiply_reduce_fusion.4
  134.9 2.6 pad_add_fusion
  138.2 2.1 convolution_convert_fusion
  140.4 2.5 convolution_convert_fusion.5
  143.5 1.6 convolution_convert_fusion.4
  145.2 2.6 multiply_reduce_fusion.22
  157.7 4.6 %all-to-all-start.3 = ((f32[16,2,1536]{2,1,0:T(2,128)}), f32[16,2,1536]{2,1,0:T(2,128)S(1)}, u32[]{:S(2)}, u32[]{:S(2)}) async-start(f32[16,2,1536]{2,1,0:T(2,128)} %reshape.316), calls=%async_computation.4 | async-start | bytes 393216 | tf_op jit(solution)/shard_map/all_to_all | solution.py:147
  165.5 1.8 scatter_custom_fusion
  168.2 4.7 %all-to-all-done.3 = f32[16,2,1536]{2,1,0:T(2,128)S(1)} async-done(((f32[16,2,1536]{2,1,0:T(2,128)}), f32[16,2,1536]{2,1,0:T(2,128)S(1)}, u32[]{:S(2)}, u32[]{:S(2)}) %all-to-all-start.3) | async-done | bytes 196640 | tf_op jit(solution)/shard_map/all_to_all | solution.py:147
  172.9 5.0 %all-to-all-start.2 = ((bf16[32,4,2304]{2,1,0:T(4,128)(2,1)}), bf16[32,4,2304]{2,1,0:T(4,128)(2,1)S(1)}, u32[]{:S(2)}, u32[]{:S(2)}) async-start(bf16[32,4,2304]{2,1,0:T(4,128)(2,1)} %all_to_all.35), calls=%async_computation.2 | async-start | bytes 1179648 | tf_op jit(solution)/shard_map/all_to_all | solution.py:123
  178.0 18.4 %all-to-all-done.2 = bf16[32,4,2304]{2,1,0:T(4,128)(2,1)S(1)} async-done(((bf16[32,4,2304]{2,1,0:T(4,128)(2,1)}), bf16[32,4,2304]{2,1,0:T(4,128)(2,1)S(1)}, u32[]{:S(2)}, u32[]{:S(2)}) %all-to-all-start.2) | async-done | bytes 589856 | tf_op jit(solution)/shard_map/all_to_all | solution.py:123
  197.8 20.5 %all_to_all.50 = f32[32,2,1536]{2,1,0:T(2,128)S(1)} all-to-all(f32[32,2,1536]{2,1,0:T(2,128)S(1)} %reshape.317), channel_id=1, replica_groups=mesh['dz'=8,'dx'=4,'fy'=8,'fc'=2] {'dz','dx'}, dimensions={0} | all-to-all | bytes 786432 | tf_op jit(solution)/shard_map/all_to_all | solution.py:147
  219.2 5.7 %all-to-all-start.5 = ((f32[32,2,1536]{2,1,0:T(2,128)}), f32[32,2,1536]{2,1,0:T(2,128)S(1)}, u32[]{:S(2)}, u32[]{:S(2)}) async-start(f32[32,2,1536]{2,1,0:T(2,128)} %broadcast_in_dim.55), calls=%async_computation.6 | async-start | bytes 786432 | tf_op jit(solution)/shard_map/all_to_all | solution.py:156
  224.9 2.4 scatter_custom_fusion.1
  227.3 9.1 %all-to-all-done.5 = f32[32,2,1536]{2,1,0:T(2,128)S(1)} async-done(((f32[32,2,1536]{2,1,0:T(2,128)}), f32[32,2,1536]{2,1,0:T(2,128)S(1)}, u32[]{:S(2)}, u32[]{:S(2)}) %all-to-all-start.5) | async-done | bytes 393248 | tf_op jit(solution)/shard_map/all_to_all | solution.py:156
  237.1 12.8 %all-to-all-start.6 = ((f32[16,2,1536]{2,1,0:T(2,128)}), f32[16,2,1536]{2,1,0:T(2,128)S(1)}, u32[]{:S(2)}, u32[]{:S(2)}) async-start(f32[16,2,1536]{2,1,0:T(2,128)} %broadcast_in_dim.57), calls=%async_computation.7 | async-start | bytes 393216 | tf_op jit(solution)/shard_map/all_to_all | solution.py:156
  251.0 9.3 %all-to-all-done.6 = f32[16,2,1536]{2,1,0:T(2,128)S(1)} async-done(((f32[16,2,1536]{2,1,0:T(2,128)}), f32[16,2,1536]{2,1,0:T(2,128)S(1)}, u32[]{:S(2)}, u32[]{:S(2)}) %all-to-all-start.6) | async-done | bytes 196640 | tf_op jit(solution)/shard_map/all_to_all | solution.py:156
  (144 shorter events, 30.8 us)
Async XLA Ops:
  10.1 31.3 %copy-start.2 = (bf16[48,1536]{1,0:T(8,128)(2,1)S(1)}, bf16[48,1536]{1,0:T(8,128)(2,1)}, u32[]{:S(2)}) copy-start(bf16[48,1536]{1,0:T(8,128)(2,1)} %param.10) | copy-start | bytes 442372
  43.1 75.0 %all-to-all-start.1 = ((bf16[16,48,1536]{2,1,0:T(8,128)(2,1)}), bf16[16,48,1536]{2,1,0:T(8,128)(2,1)}, u32[]{:S(2)}, u32[]{:S(2)}) async-start(bf16[16,48,1536]{2,1,0:T(8,128)(2,1)} %stack.2), calls=%async_computation.1 | async-start | bytes 4718592 | tf_op jit(solution)/shard_map/all_to_all | solution.py:95
  52.8 87.6 %all-gather.2.cloned.1.call-start = ((), (), s32[]{:S(2)}) async-start(), calls=%async_computation.8 | async-start | bytes 2506752 | tf_op jit(solution)/shard_map/all_gather | solution.py:116
  53.5 143.0 %reduce-scatter.2.cloned.1.call-start = ((), (), s32[]{:S(2)}) async-start(), calls=%async_computation.9 | async-start | bytes 2506752 | tf_op jit(solution)/shard_map/reduce_scatter | solution.py:105
  54.9 78.5 %copy-start.15 = (f32[128]{0:T(128)}, f32[128]{0:T(128)S(1)}, u32[]{:S(2)}) copy-start(f32[128]{0:T(128)S(1)} %get-tuple-element.116) | copy-start | bytes 1540
  54.9 78.5 %copy-start.16 = (f32[128]{0:T(128)}, f32[128]{0:T(128)S(1)}, u32[]{:S(2)}) copy-start(f32[128]{0:T(128)S(1)} %get-tuple-element.117) | copy-start | bytes 1540
  54.9 78.5 %copy-start.17 = (f32[128]{0:T(128)}, f32[128]{0:T(128)S(1)}, u32[]{:S(2)}) copy-start(f32[128]{0:T(128)S(1)} %get-tuple-element.118) | copy-start | bytes 1540
  54.9 78.5 %copy-start.18 = (f32[128]{0:T(128)}, f32[128]{0:T(128)S(1)}, u32[]{:S(2)}) copy-start(f32[128]{0:T(128)S(1)} %get-tuple-element.119) | copy-start | bytes 1540
  55.0 78.5 %copy-start.19 = (f32[128]{0:T(128)}, f32[128]{0:T(128)S(1)}, u32[]{:S(2)}) copy-start(f32[128]{0:T(128)S(1)} %get-tuple-element.120) | copy-start | bytes 1540
  55.0 78.5 %copy-start.20 = (f32[128]{0:T(128)}, f32[128]{0:T(128)S(1)}, u32[]{:S(2)}) copy-start(f32[128]{0:T(128)S(1)} %get-tuple-element.121) | copy-start | bytes 1540
  55.0 79.2 %copy-start.21 = (f32[128]{0:T(128)}, f32[128]{0:T(128)S(1)}, u32[]{:S(2)}) copy-start(f32[128]{0:T(128)S(1)} %get-tuple-element.122) | copy-start | bytes 1540
  55.0 79.2 %copy-start.22 = (f32[128]{0:T(128)}, f32[128]{0:T(128)S(1)}, u32[]{:S(2)}) copy-start(f32[128]{0:T(128)S(1)} %get-tuple-element.123) | copy-start | bytes 1540
  55.0 79.2 %copy-start.23 = (f32[128]{0:T(128)}, f32[128]{0:T(128)S(1)}, u32[]{:S(2)}) copy-start(f32[128]{0:T(128)S(1)} %get-tuple-element.124) | copy-start | bytes 1540
  56.8 61.3 %copy-start.3 = (bf16[128,768]{0,1:T(8,128)(2,1)}, bf16[128,768]{0,1:T(8,128)(2,1)S(1)}, u32[]{:S(2)}) copy-start(bf16[128,768]{0,1:T(8,128)(2,1)S(1)} %copy.47) | copy-start | bytes 589828
  58.1 62.1 %copy-start.26 = (f32[8,128]{1,0:T(8,128)}, f32[8,128]{1,0:T(8,128)S(1)}, u32[]{:S(2)}) copy-start(f32[8,128]{1,0:T(8,128)S(1)} %get-tuple-element.144) | copy-start | bytes 12292
  58.6 61.6 %copy-start.1 = (bf16[128,1536]{1,0:T(8,128)(2,1)S(1)}, bf16[128,1536]{1,0:T(8,128)(2,1)}, u32[]{:S(2)}) copy-start(bf16[128,1536]{1,0:T(8,128)(2,1)} %param.12) | copy-start | bytes 1179652
  143.5 13.0 %copy-start.9 = (f32[1536]{0:T(1024)S(1)}, f32[1536]{0:T(1024)}, u32[]{:S(2)}) copy-start(f32[1536]{0:T(1024)} %get-tuple-element.10) | copy-start | bytes 18436
  143.5 13.0 %copy-start.8 = (f32[1536]{0:T(1024)S(1)}, f32[1536]{0:T(1024)}, u32[]{:S(2)}) copy-start(f32[1536]{0:T(1024)} %get-tuple-element.11) | copy-start | bytes 18436
  143.5 13.0 %copy-start.7 = (f32[1536]{0:T(1024)S(1)}, f32[1536]{0:T(1024)}, u32[]{:S(2)}) copy-start(f32[1536]{0:T(1024)} %get-tuple-element.12) | copy-start | bytes 18436
  143.5 13.1 %copy-start.6 = (f32[1536]{0:T(1024)S(1)}, f32[1536]{0:T(1024)}, u32[]{:S(2)}) copy-start(f32[1536]{0:T(1024)} %get-tuple-element.13) | copy-start | bytes 18436
  157.7 15.2 %all-to-all-start.3 = ((f32[16,2,1536]{2,1,0:T(2,128)}), f32[16,2,1536]{2,1,0:T(2,128)S(1)}, u32[]{:S(2)}, u32[]{:S(2)}) async-start(f32[16,2,1536]{2,1,0:T(2,128)} %reshape.316), calls=%async_computation.4 | async-start | bytes 393216 | tf_op jit(solution)/shard_map/all_to_all | solution.py:147
  172.9 23.4 %all-to-all-start.2 = ((bf16[32,4,2304]{2,1,0:T(4,128)(2,1)}), bf16[32,4,2304]{2,1,0:T(4,128)(2,1)S(1)}, u32[]{:S(2)}, u32[]{:S(2)}) async-start(bf16[32,4,2304]{2,1,0:T(4,128)(2,1)} %all_to_all.35), calls=%async_computation.2 | async-start | bytes 1179648 | tf_op jit(solution)/shard_map/all_to_all | solution.py:123
  219.2 17.2 %all-to-all-start.5 = ((f32[32,2,1536]{2,1,0:T(2,128)}), f32[32,2,1536]{2,1,0:T(2,128)S(1)}, u32[]{:S(2)}, u32[]{:S(2)}) async-start(f32[32,2,1536]{2,1,0:T(2,128)} %broadcast_in_dim.55), calls=%async_computation.6 | async-start | bytes 786432 | tf_op jit(solution)/shard_map/all_to_all | solution.py:156
  237.1 23.1 %all-to-all-start.6 = ((f32[16,2,1536]{2,1,0:T(2,128)}), f32[16,2,1536]{2,1,0:T(2,128)S(1)}, u32[]{:S(2)}, u32[]{:S(2)}) async-start(f32[16,2,1536]{2,1,0:T(2,128)} %broadcast_in_dim.57), calls=%async_computation.7 | async-start | bytes 393216 | tf_op jit(solution)/shard_map/all_to_all | solution.py:156
  (11 other events, 102.5 us)
Sparse Core Ops, SparseCore 0:
  55.7 64.0 all-gather.1
  140.5 54.9 reduce-scatter.1
